TPU v7x, 32 devices: a whole 2x2x4 slice. The times are simulated.
32 devices in a mesh: rep: 2 (over x), seq: 4 (over y, core), head: 4 (over z).
Axes of the slice: x: 2, y: 2, z: 4, core: 2. Of those that a mesh axis runs over, the one named last changes fastest.
Arguments:
- query_rows: bfloat16 [2048, 8192], P(('rep', 'seq'), 'head'), parts along dimension 0, may hold values from -128 to 128
- span_kv: bfloat16 [2, 2048, 1024], P(None, ('rep', 'seq'), 'head'), parts along dimension 1, may hold values from -6 to 6
- cache_kv: bfloat16 [2, 4096, 1024], P(None, ('rep', 'seq'), 'head'), parts along dimension 1, may hold values from -6 to 6
- cache_len: int32 [8], P(('rep', 'seq')), parts along dimension 0, may hold values from 1 to 512, 1024 in all
Outputs:
- attended: bfloat16 [2048, 8192], P(('rep', 'seq'), 'head'), parts along dimension 0
There are 2 independent parts, one for each index of `rep`. A program takes and returns all parts, laid end to end along the dimension named above; each array names one. Nothing has to cross between parts.
Inputs may be any that keep to these rules, and one draw needn't show every extreme that they name: `cache_len`: the earlier prompt is the filled slots of the instances in order; every instance has at least one filled slot and some instance is full.
All inputs are finite; a program needn't handle non-finite values. No bound on the sum of `cache_len` on one device may be relied on, other than what follows from the above.
Results may differ from a plain program's by a relative error of at most 0.007.
Values may be sent and summed in bfloat16 or wider, within the bound.
No kernel may reach another device: no remote copies, remote signals or barrier semaphores. Data moves between devices by JAX's collectives and lax.ppermute only.
A program may use at most 64 MiB of HBM per device.

v0:
```python
import functools

import jax
import jax.numpy as jnp
from jax import lax
from jax.experimental import pallas as pl
from jax.experimental.pallas import tpu as pltpu
from jax.sharding import PartitionSpec as P

HD = 128
NEG = -1e30
BK = 256


def step_kernel(sc_ref, q_ref, *refs, ninst, t_rows, group, first, last):
    inst_refs = [refs[4 * i:4 * i + 4] for i in range(ninst)]
    rest = refs[4 * ninst:]
    if first:
        state_in = None
    else:
        state_in, rest = rest[:3], rest[3:]
    if first and last:
        o_refs, (qs_ref, m_ref, l_ref, acc_ref) = rest[:-4], rest[-4:]
    else:
        o_refs, qs_ref = rest[:-1], rest[-1]
        if last:
            m_ref, l_ref, acc_ref = state_in
        else:
            m_ref, l_ref, acc_ref = o_refs
    own = sc_ref[2 * ninst]
    scale = HD ** (-0.5) * 1.4426950408889634
    rows_all = group * t_rows
    reps = BK // 128
    for g in range(group):
        qs_ref[g * t_rows:(g + 1) * t_rows, :] = q_ref[:, g * HD:(g + 1) * HD]
    if first:
        m_ref[...] = jnp.full(m_ref.shape, NEG, jnp.float32)
        l_ref[...] = jnp.zeros(l_ref.shape, jnp.float32)
        acc_ref[...] = jnp.zeros(acc_ref.shape, jnp.float32)
    elif not last:
        m_ref[...] = state_in[0][...]
        l_ref[...] = state_in[1][...]
        acc_ref[...] = state_in[2][...]

    def step(start, k_ref, v_ref, limit=None, causal=False):
        k = k_ref[pl.ds(start, BK), :]
        v = v_ref[pl.ds(start, BK), :]
        s = lax.dot_general(qs_ref[...], k, (((1,), (1,)), ((), ())), preferred_element_type=jnp.float32) * scale
        if limit is not None:
            mask = lax.broadcasted_iota(jnp.int32, (rows_all, BK), 1) < limit
            s = jnp.where(mask, s, NEG)
        if causal:
            cols = lax.broadcasted_iota(jnp.int32, (t_rows, BK), 1) + start
            rows = lax.broadcasted_iota(jnp.int32, (t_rows, BK), 0)
            mask = jnp.concatenate([cols <= rows] * group, axis=0)
            s = jnp.where(mask, s, NEG)
        m_prev = m_ref[...]
        m_new = jnp.maximum(m_prev, jnp.max(s, axis=1, keepdims=True))
        alpha = jnp.exp2(m_prev - m_new)
        m_wide = m_new if reps == 1 else jnp.concatenate([m_new] * reps, axis=1)
        p = jnp.exp2(s - m_wide)
        p_sum = p[:, :128]
        for r in range(1, reps):
            p_sum = p_sum + p[:, r * 128:(r + 1) * 128]
        l_ref[...] = alpha * l_ref[...] + p_sum
        acc_ref[...] = alpha * acc_ref[...] + jnp.dot(p.astype(v.dtype), v, preferred_element_type=jnp.float32)
        m_ref[...] = m_new

    for i, (ck_ref, cv_ref, sk_ref, sv_ref) in enumerate(inst_refs):
        length = sc_ref[i]
        origin = sc_ref[ninst + i]
        n_full = length // BK
        rem = length - n_full * BK

        def loop_body(b, c, ck_ref=ck_ref, cv_ref=cv_ref):
            step(pl.multiple_of(b * BK, BK), ck_ref, cv_ref)
            return c

        lax.fori_loop(0, n_full, loop_body, 0)

        @pl.when(rem > 0)
        def _(ck_ref=ck_ref, cv_ref=cv_ref, n_full=n_full, rem=rem):
            step(pl.multiple_of(n_full * BK, BK), ck_ref, cv_ref, limit=rem)

        @pl.when(origin < own)
        def _(sk_ref=sk_ref, sv_ref=sv_ref):
            for d in range(t_rows // BK):
                step(d * BK, sk_ref, sv_ref)

        @pl.when(origin == own)
        def _(sk_ref=sk_ref, sv_ref=sv_ref):
            for d in range(t_rows // BK):
                step(d * BK, sk_ref, sv_ref, causal=True)

    if last:
        (o_ref,) = o_refs
        out = acc_ref[...] / jnp.sum(l_ref[...], axis=1, keepdims=True)
        for g in range(group):
            o_ref[:, g * HD:(g + 1) * HD] = out[g * t_rows:(g + 1) * t_rows].astype(o_ref.dtype)


def attn_call(sc, q, insts, rows, state, first, last):
    t_rows, q_width = q.shape
    kv_width = insts[0][0].shape[2]
    kv_local = kv_width // HD
    group = q_width // kv_width
    c_rows, s_rows = rows
    rows_all = group * t_rows
    ninst = len(insts)
    kernel = functools.partial(step_kernel, ninst=ninst, t_rows=t_rows, group=group, first=first, last=last)
    st_spec = pl.BlockSpec((rows_all, 128), lambda k, *_: (k, 0))
    st_shape = jax.ShapeDtypeStruct((kv_local * rows_all, 128), jnp.float32)
    in_specs = [pl.BlockSpec((t_rows, group * HD), lambda k, *_: (0, k))]
    args = [sc, q]
    for cache, span, srow in insts:
        in_specs += [
            pl.BlockSpec((None, c_rows, HD), lambda k, *_: (0, 0, k)),
            pl.BlockSpec((None, c_rows, HD), lambda k, *_: (1, 0, k)),
            pl.BlockSpec((None, s_rows, HD), lambda k, *_, srow=srow: (0, srow, k)),
            pl.BlockSpec((None, s_rows, HD), lambda k, *_, srow=srow: (1, srow, k)),
        ]
        args += [cache, cache, span, span]
    if not first:
        in_specs += [st_spec] * 3
        args += list(state)
    if last:
        out_specs = pl.BlockSpec((t_rows, group * HD), lambda k, *_: (0, k))
        out_shape = jax.ShapeDtypeStruct((t_rows, q_width), q.dtype)
    else:
        out_specs = [st_spec] * 3
        out_shape = [st_shape] * 3
    keys = ninst * (c_rows + s_rows)
    heads = kv_local * group
    cost = pl.CostEstimate(
        flops=4 * heads * t_rows * keys * HD,
        transcendentals=heads * t_rows * keys,
        bytes_accessed=2 * t_rows * q_width + 4 * keys * kv_width + 24 * kv_local * rows_all * 128,
    )
    grid_spec = pltpu.PrefetchScalarGridSpec(
        num_scalar_prefetch=1,
        grid=(kv_local,),
        in_specs=in_specs,
        out_specs=out_specs,
        scratch_shapes=[pltpu.VMEM((rows_all, HD), q.dtype)] + ([
            pltpu.VMEM((rows_all, 128), jnp.float32),
            pltpu.VMEM((rows_all, 128), jnp.float32),
            pltpu.VMEM((rows_all, HD), jnp.float32),
        ] if first and last else []),
    )
    return pl.pallas_call(
        kernel,
        out_shape=out_shape,
        grid_spec=grid_spec,
        compiler_params=pltpu.CompilerParams(dimension_semantics=("arbitrary",)),
        cost_estimate=cost,
    )(*args)


def chain_need(n, first_pairs, hops):
    need = []
    for k in range(len(hops)):
        keep = []
        for src in range(n):
            origin = first_pairs[src]
            dst = src
            for j in range(k + 1):
                dst = hops[j](dst)
            later = [dst, dst ^ 1]
            d = dst
            for j in range(k + 1, len(hops)):
                d = hops[j](d)
                later += [d, d ^ 1]
            if any(x > origin for x in later):
                keep.append(src)
        need.append(keep)
    return need


def body(query_rows, span_kv, cache_kv, cache_len):
    n = lax.psum(1, "seq")
    own = lax.axis_index("seq").astype(jnp.int32)
    n_chips = n // 2
    c_rows = cache_kv.shape[1]
    s_rows = span_kv.shape[1]
    kv_width = cache_kv.shape[2]
    length = cache_len.reshape(())
    tag = jnp.zeros((2, 16, kv_width), cache_kv.dtype)
    tag = tag.at[0, 0, 0].set((length // 64).astype(cache_kv.dtype))
    tag = tag.at[0, 0, 1].set((length % 64).astype(cache_kv.dtype))
    merged = jnp.concatenate([cache_kv, span_kv, tag], axis=1)
    srow = c_rows // s_rows

    def send(x, fn):
        return lax.ppermute(x, "seq", [(i, fn(i)) for i in range(n)])

    def length_of(blk):
        hi = blk[0, c_rows + s_rows, 0].astype(jnp.int32)
        lo = blk[0, c_rows + s_rows, 1].astype(jnp.int32)
        return hi * 64 + lo

    calls = [0]

    def run(phase, state):
        lens = [jnp.asarray(ln, jnp.int32).reshape(1) for _, ln, _ in phase]
        origins = [jnp.asarray(o, jnp.int32).reshape(1) for _, _, o in phase]
        sc = jnp.concatenate(lens + origins + [own.reshape(1)]).astype(jnp.int32)
        insts = [b for b, _, _ in phase]
        first = calls[0] == 0
        calls[0] += 1
        return attn_call(sc, query_rows, insts, (c_rows, s_rows), state, first=first, last=(calls[0] == n_chips))

    part = send(merged, lambda i: i ^ 1)
    k_right = n_chips // 2
    k_left = n_chips - 1 - k_right
    hops = []
    for sign, count in ((2, k_right), (-2, k_left)):
        blk = merged
        for k in range(1, count + 1):
            blk = send(blk, lambda i, sign=sign: (i + sign) % n)
            hops.append((blk, sign, k))
    state = run([((cache_kv, span_kv, 0), length, own), ((part, part, srow), length_of(part), own ^ 1)], None)
    for blk, sign, k in hops:
        state, blk = lax.optimization_barrier((state, blk))
        origin = (own - sign * k) % n
        fwd = send(blk, lambda i: i ^ 1)
        state = run([((blk, blk, srow), length_of(blk), origin), ((fwd, fwd, srow), length_of(fwd), origin ^ 1)], state)
    return state


def solution(mesh):
    in_specs = (
        P(("rep", "seq"), "head"),
        P(None, ("rep", "seq"), "head"),
        P(None, ("rep", "seq"), "head"),
        P(("rep", "seq")),
    )
    out_specs = P(("rep", "seq"), "head")
    return jax.shard_map(body, mesh=mesh, in_specs=in_specs, out_specs=out_specs, check_vma=False)
```

profile of v0, /device:TPU:13, one launch (start us, length us, event | category | flops | bytes accessed | tf_op | source)
XLA Modules:
  0.0 44.2 jit_solution(13625930604717018544)
XLA Ops:
  0.7 0.1 scatter.9
  0.8 1.2 %pad_maximum_fusion = bf16[2,784,256]{2,1,0:T(8,128)(2,1)S(1)} fusion(bf16[2,16,256]{2,1,0:T(8,128)(2,1)S(1)} %scatter.9, bf16[2,256,256]{2,1,0:T(8,128)(2,1)} %refs_3_.1, bf16[2,512,256]{2,1,0:T(8,128)(2,1)} %refs_1_.1), kind=kLoop, calls=%fused_computation | loop fusion | flops 2408448 | bytes 1605632 | tf_op jit(solution)/shard_map/concatenate | solution.py:190
  2.0 0.7 %collective-permute-start = (bf16[2,784,256]{2,1,0:T(8,128)(2,1)S(1)}, bf16[2,784,256]{2,1,0:T(8,128)(2,1)S(1)}, u32[]{:S(2)}, u32[]{:S(2)}) collective-permute-start(bf16[2,784,256]{2,1,0:T(8,128)(2,1)S(1)} %pad_maximum_fusion), channel_id=1, source_target_pairs={{0,4},{4,0},{8,12},{12,8},{1,5},{5,1},{9,13},{13,9},{2,6},{6,2},{1... | collective-permute-start | bytes 2408456 | tf_op jit(solution)/shard_map/ppermute | solution.py:194
  2.8 0.2 collective-permute-start.1
  3.0 1.7 %collective-permute-done.refs_4_.refs_5_.refs_6_.refs_7_ = bf16[2,784,256]{2,1,0:T(8,128)(2,1)S(1)} collective-permute-done((bf16[2,784,256]{2,1,0:T(8,128)(2,1)S(1)}, bf16[2,784,256]{2,1,0:T(8,128)(2,1)S(1)}, u32[]{:S(2)}, u32[]{:S(2)}) %collective-permute-start) | collective-permute-done | bytes 802848 | tf_op jit(solution)/shard_map/ppermute | solution.py:194
  4.7 0.0 copy-start.2
  4.7 0.8 %fusion.2 = (bf16[1,1,1]{2,1,0:T(2,128)(2,1)}, bf16[1,1,1]{2,1,0:T(2,128)(2,1)}) fusion(bf16[2,784,256]{2,1,0:T(8,128)(2,1)S(1)} %collective-permute-done.refs_4_.refs_5_.refs_6_.refs_7_), kind=kLoop, calls=%fused_computation.3 | loop fusion | bytes 8 | tf_op jit(solution)/shard_map/slice | solution.py:198
  6.7 0.6 %concatenate.15.sc_ref = s32[5]{0:T(128)} concatenate(s32[1]{0:T(128)} %copy.6, s32[1]{0:T(128)} %bitcast.3, s32[1]{0:T(128)} %bitcast.4, s32[1]{0:T(128)} %bitcast.5, s32[1]{0:T(128)} %bitcast.4), dimensions={0} | concatenate | bytes 40 | tf_op jit(solution)/shard_map/concatenate | solution.py:206
  7.3 0.0 copy-done.2
  7.4 11.9 %shard_map.46 = (f32[4096,128]{1,0:T(8,128)}, f32[4096,128]{1,0:T(8,128)}, f32[4096,128]{1,0:T(8,128)}) custom-call(s32[5]{0:T(128)} %concatenate.15.sc_ref, bf16[256,2048]{1,0:T(8,128)(2,1)} %q_ref.3, bf16[2,512,256]{2,1,0:T(8,128)(2,1)} %refs_1_.1, bf16[2,512,256]{2,1,0:T(8,128)(2,1)} %refs_1_.1, bf16[2,256,256]{2,1,0:T(8,128)(2,1)} %refs_3_.1, ...), custom_call_target="tpu_custom_call" | custom-call | flops 3221225472 | bytes 15204352 | tf_op jit(solution)/shard_map/pallas_call | solution.py:150
  19.3 3.0 %collective-permute-done.1.refs_0_.refs_1_.refs_2_.refs_3_ = bf16[2,784,256]{2,1,0:T(8,128)(2,1)S(1)} collective-permute-done((bf16[2,784,256]{2,1,0:T(8,128)(2,1)S(1)}, bf16[2,784,256]{2,1,0:T(8,128)(2,1)S(1)}, u32[]{:S(2)}, u32[]{:S(2)}) %collective-permute-start.1) | collective-permute-done | bytes 802848 | tf_op jit(solution)/shard_map/ppermute | solution.py:194
  22.2 0.0 copy-start
  22.2 0.8 %collective-permute-start.2 = (bf16[2,784,256]{2,1,0:T(8,128)(2,1)S(1)}, bf16[2,784,256]{2,1,0:T(8,128)(2,1)S(1)}, u32[]{:S(2)}, u32[]{:S(2)}) collective-permute-start(bf16[2,784,256]{2,1,0:T(8,128)(2,1)S(1)} %collective-permute-done.1.refs_0_.refs_1_.refs_2_.refs_3_), channel_id=1, source_target_pairs={{0,4},{4,0},{8,12},{12,8},{1,5},{5,1},{9,13},{13,9},{2,6},{6,2},{1... | collective-permute-start | bytes 2408456 | tf_op jit(solution)/shard_map/ppermute | solution.py:194
  23.1 0.6 %fusion.1 = (bf16[1,1,1]{2,1,0:T(2,128)(2,1)}, bf16[1,1,1]{2,1,0:T(2,128)(2,1)}) fusion(bf16[2,784,256]{2,1,0:T(8,128)(2,1)S(1)} %collective-permute-done.1.refs_0_.refs_1_.refs_2_.refs_3_), kind=kLoop, calls=%fused_computation.2 | loop fusion | bytes 8 | tf_op jit(solution)/shard_map/slice | solution.py:198
  25.0 0.1 collective-permute-done.2.refs_4_.refs_5_.refs_6_.refs_7_
  25.0 0.0 copy-start.1
  25.0 0.7 %fusion = (bf16[1,1,1]{2,1,0:T(2,128)(2,1)}, bf16[1,1,1]{2,1,0:T(2,128)(2,1)}) fusion(bf16[2,784,256]{2,1,0:T(8,128)(2,1)S(1)} %collective-permute-done.2.refs_4_.refs_5_.refs_6_.refs_7_), kind=kLoop, calls=%fused_computation.1 | loop fusion | bytes 8 | tf_op jit(solution)/shard_map/slice | solution.py:198
  27.0 0.6 %concatenate.16.sc_ref = s32[5]{0:T(128)} concatenate(s32[1]{0:T(128)} %bitcast.6, s32[1]{0:T(128)} %bitcast.7, s32[1]{0:T(128)} %bitcast.8, s32[1]{0:T(128)} %bitcast.9, s32[1]{0:T(128)} %bitcast.4), dimensions={0} | concatenate | bytes 40 | tf_op jit(solution)/shard_map/concatenate | solution.py:206
  27.6 0.0 copy-done
  27.7 0.0 copy-done.1
  27.7 16.5 %shard_map.47 = bf16[256,2048]{1,0:T(8,128)(2,1)} custom-call(s32[5]{0:T(128)} %concatenate.16.sc_ref, bf16[256,2048]{1,0:T(8,128)(2,1)} %q_ref.3, bf16[2,784,256]{2,1,0:T(8,128)(2,1)} %copy-done, bf16[2,784,256]{2,1,0:T(8,128)(2,1)} %copy-done, bf16[2,784,256]{2,1,0:T(8,128)(2,1)} %copy-done, bf16[2,784,256]{2,1,0:T(8,128)(2,1)} %copy-done, ...), custom_call_target="tpu_custom_call" | custom-call | flops 3221225472 | bytes 15204352 | tf_op jit(solution)/shard_map/pallas_call | solution.py:150
  (1 shorter events, 0.0 us)
Async XLA Ops:
  2.0 2.7 %collective-permute-start = (bf16[2,784,256]{2,1,0:T(8,128)(2,1)S(1)}, bf16[2,784,256]{2,1,0:T(8,128)(2,1)S(1)}, u32[]{:S(2)}, u32[]{:S(2)}) collective-permute-start(bf16[2,784,256]{2,1,0:T(8,128)(2,1)S(1)} %pad_maximum_fusion), channel_id=1, source_target_pairs={{0,4},{4,0},{8,12},{12,8},{1,5},{5,1},{9,13},{13,9},{2,6},{6,2},{1... | collective-permute-start | bytes 2408456 | tf_op jit(solution)/shard_map/ppermute | solution.py:194
  2.8 19.5 %collective-permute-start.1 = (bf16[2,784,256]{2,1,0:T(8,128)(2,1)S(1)}, bf16[2,784,256]{2,1,0:T(8,128)(2,1)S(1)}, u32[]{:S(2)}, u32[]{:S(2)}) collective-permute-start(bf16[2,784,256]{2,1,0:T(8,128)(2,1)S(1)} %pad_maximum_fusion), channel_id=1, source_target_pairs={{0,8},{4,12},{8,0},{12,4},{1,9},{5,13},{9,1},{13,5},{2,10},{6,14},... | collective-permute-start | bytes 2408456 | tf_op jit(solution)/shard_map/ppermute | solution.py:194
  4.7 2.7 %copy-start.2 = (bf16[2,784,256]{2,1,0:T(8,128)(2,1)}, bf16[2,784,256]{2,1,0:T(8,128)(2,1)S(1)}, u32[]{:S(2)}) copy-start(bf16[2,784,256]{2,1,0:T(8,128)(2,1)S(1)} %collective-permute-done.refs_4_.refs_5_.refs_6_.refs_7_) | copy-start | bytes 2408452
  22.2 5.4 %copy-start = (bf16[2,784,256]{2,1,0:T(8,128)(2,1)}, bf16[2,784,256]{2,1,0:T(8,128)(2,1)S(1)}, u32[]{:S(2)}) copy-start(bf16[2,784,256]{2,1,0:T(8,128)(2,1)S(1)} %collective-permute-done.1.refs_0_.refs_1_.refs_2_.refs_3_) | copy-start | bytes 2408452
  22.2 2.8 %collective-permute-start.2 = (bf16[2,784,256]{2,1,0:T(8,128)(2,1)S(1)}, bf16[2,784,256]{2,1,0:T(8,128)(2,1)S(1)}, u32[]{:S(2)}, u32[]{:S(2)}) collective-permute-start(bf16[2,784,256]{2,1,0:T(8,128)(2,1)S(1)} %collective-permute-done.1.refs_0_.refs_1_.refs_2_.refs_3_), channel_id=1, source_target_pairs={{0,4},{4,0},{8,12},{12,8},{1,5},{5,1},{9,13},{13,9},{2,6},{6,2},{1... | collective-permute-start | bytes 2408456 | tf_op jit(solution)/shard_map/ppermute | solution.py:194
  25.0 2.6 %copy-start.1 = (bf16[2,784,256]{2,1,0:T(8,128)(2,1)}, bf16[2,784,256]{2,1,0:T(8,128)(2,1)S(1)}, u32[]{:S(2)}) copy-start(bf16[2,784,256]{2,1,0:T(8,128)(2,1)S(1)} %collective-permute-done.2.refs_4_.refs_5_.refs_6_.refs_7_) | copy-start | bytes 2408452
where the time goes:
time: 43.5 us; the launch traced here: 44.2 us
  Pallas kernels  28.4 us (65%)
  waiting for transfers between devices  4.71 us (11%)
  between operations  4.61 us (11%)
  local copies, waits for them, and re-layouts  3.4 us (8%)
  starting transfers between devices  1.83 us (4%)
  other arithmetic  1.18 us (3%)
    pallas_call x2, Pallas kernels, attn_call(): pl.pallas_call(kernel, out_shape=out_shape, grid_spec=grid_spec, compiler...  28.4 us
    ppermute x3, waiting for transfers between devices, send(): return lax.ppermute(x, 'seq', [(i, fn(i)) for i in range(n)])  4.71 us
    slice x3, local copies, waits for them, and re-layouts, length_of(): lo = blk[0, c_rows + s_rows, 1].astype(jnp.int32)  2.01 us
    ppermute x3, starting transfers between devices, send(): return lax.ppermute(x, 'seq', [(i, fn(i)) for i in range(n)])  1.83 us
    concatenate x2, local copies, waits for them, and re-layouts, run(): sc = jnp.concatenate(lens + origins + [own.reshape(1)]).astype(jnp.int32)  1.26 us
    concatenate x1, other arithmetic, body(): merged = jnp.concatenate([cache_kv, span_kv, tag], axis=1)  1.18 us
  transfers between devices with their start and end apart: 3, of which 3 were waited for; matrix products, arithmetic and copies ran while one was open for 4% of the time, Pallas kernels for 27%

commit v1 on v0

--- a/solution.py
+++ b/solution.py
@@ -10,11 +10,13 @@
 HD = 128
 NEG = -1e30
 BK = 256
-
-
-def step_kernel(sc_ref, q_ref, *refs, ninst, t_rows, group, first, last):
-    inst_refs = [refs[4 * i:4 * i + 4] for i in range(ninst)]
-    rest = refs[4 * ninst:]
+VMEM_LIMIT = 64 * 1024 * 1024
+
+
+def step_kernel(sc_ref, q_ref, *refs, ninst, srows, t_rows, group, first, last):
+    hbm_refs = refs[:2 * ninst]
+    rest = refs[2 * ninst:-2]
+    kv_buf, sem = refs[-2:]
     if first:
         state_in = None
     else:
@@ -31,8 +33,28 @@
     scale = HD ** (-0.5) * 1.4426950408889634
     rows_all = group * t_rows
     reps = BK // 128
+    head = pl.program_id(0)
+    c_rows = kv_buf.shape[2] - t_rows
+    copies = []
+    for i in range(ninst):
+        cache_hbm, span_hbm = hbm_refs[2 * i], hbm_refs[2 * i + 1]
+        cols = pl.ds(pl.multiple_of(head * HD, HD), HD)
+        for j in range(2):
+            copies.append(pltpu.make_async_copy(
+                cache_hbm.at[j, pl.ds(0, c_rows), cols], kv_buf.at[i, j, pl.ds(0, c_rows)], sem.at[i, j, 0]))
+            copies.append(pltpu.make_async_copy(
+                span_hbm.at[j, pl.ds(srows[i] * t_rows, t_rows), cols], kv_buf.at[i, j, pl.ds(c_rows, t_rows)],
+                sem.at[i, j, 1]))
+    for cp in copies:
+        cp.start()
     for g in range(group):
         qs_ref[g * t_rows:(g + 1) * t_rows, :] = q_ref[:, g * HD:(g + 1) * HD]
+    for cp in copies:
+        cp.wait()
+    inst_refs = []
+    for i in range(ninst):
+        k_all, v_all = kv_buf.at[i, 0], kv_buf.at[i, 1]
+        inst_refs.append((k_all, v_all, k_all.at[pl.ds(c_rows, t_rows)], v_all.at[pl.ds(c_rows, t_rows)]))
     if first:
         m_ref[...] = jnp.full(m_ref.shape, NEG, jnp.float32)
         l_ref[...] = jnp.zeros(l_ref.shape, jnp.float32)
@@ -107,19 +129,15 @@
     c_rows, s_rows = rows
     rows_all = group * t_rows
     ninst = len(insts)
-    kernel = functools.partial(step_kernel, ninst=ninst, t_rows=t_rows, group=group, first=first, last=last)
+    kernel = functools.partial(step_kernel, ninst=ninst, srows=tuple(sr for _, _, sr in insts), t_rows=t_rows,
+                               group=group, first=first, last=last)
     st_spec = pl.BlockSpec((rows_all, 128), lambda k, *_: (k, 0))
     st_shape = jax.ShapeDtypeStruct((kv_local * rows_all, 128), jnp.float32)
     in_specs = [pl.BlockSpec((t_rows, group * HD), lambda k, *_: (0, k))]
     args = [sc, q]
     for cache, span, srow in insts:
-        in_specs += [
-            pl.BlockSpec((None, c_rows, HD), lambda k, *_: (0, 0, k)),
-            pl.BlockSpec((None, c_rows, HD), lambda k, *_: (1, 0, k)),
-            pl.BlockSpec((None, s_rows, HD), lambda k, *_, srow=srow: (0, srow, k)),
-            pl.BlockSpec((None, s_rows, HD), lambda k, *_, srow=srow: (1, srow, k)),
-        ]
-        args += [cache, cache, span, span]
+        in_specs += [pl.BlockSpec(memory_space=pl.ANY), pl.BlockSpec(memory_space=pl.ANY)]
+        args += [cache, span]
     if not first:
         in_specs += [st_spec] * 3
         args += list(state)
@@ -145,13 +163,16 @@
             pltpu.VMEM((rows_all, 128), jnp.float32),
             pltpu.VMEM((rows_all, 128), jnp.float32),
             pltpu.VMEM((rows_all, HD), jnp.float32),
-        ] if first and last else []),
+        ] if first and last else []) + [
+            pltpu.VMEM((ninst, 2, c_rows + s_rows, HD), q.dtype),
+            pltpu.SemaphoreType.DMA((ninst, 2, 2)),
+        ],
     )
     return pl.pallas_call(
         kernel,
         out_shape=out_shape,
         grid_spec=grid_spec,
-        compiler_params=pltpu.CompilerParams(dimension_semantics=("arbitrary",)),
+        compiler_params=pltpu.CompilerParams(dimension_semantics=("arbitrary",), vmem_limit_bytes=VMEM_LIMIT),
         cost_estimate=cost,
     )(*args)
 

time: 43.5 us -> 49.2 us (1.13); the launches traced: 44.2 us -> 48.8 us
  Pallas kernels: 28.4 us -> 33.4 us
  waiting for transfers between devices: 4.71 us -> 1.92 us
  local copies, waits for them, and re-layouts: 3.4 us -> 5.72 us
  other arithmetic: 1.18 us -> 2.07 us
  starting transfers between devices: 1.83 us -> 0.97 us
    pallas_call x2, Pallas kernels: 28.4 us -> 33.4 us  [attn_call(): pl.pallas_call(kernel, out_shape=out_shape, grid_spec=grid_spec, compiler...]
    ppermute x3, waiting for transfers between devices: 4.71 us -> 1.92 us  [send(): return lax.ppermute(x, 'seq', [(i, fn(i)) for i in range(n)])]
    unnamed x6 -> x4, local copies, waits for them, and re-layouts: 0.01 us -> 1.79 us
    concatenate x1, other arithmetic: 1.18 us -> 2.07 us  [body(): merged = jnp.concatenate([cache_kv, span_kv, tag], axis=1)]
    ppermute x3, starting transfers between devices: 1.83 us -> 0.97 us  [send(): return lax.ppermute(x, 'seq', [(i, fn(i)) for i in range(n)])]
    slice x3, local copies, waits for them, and re-layouts: 2.01 us -> 2.53 us  [length_of(): lo = blk[0, c_rows + s_rows, 1].astype(jnp.int32)]
  transfers between devices with their start and end apart: 3 -> 3, of which waited for: 3 -> 1; matrix products, arithmetic and copies ran while one was open for 4% -> 5% of each run, Pallas kernels for 27% -> 34%
where the time goes in v1:
time: 49.2 us; the launch traced here: 48.8 us
  Pallas kernels  33.4 us (68%)
  local copies, waits for them, and re-layouts  5.72 us (12%)
  between operations  4.71 us (10%)
  other arithmetic  2.07 us (4%)
  waiting for transfers between devices  1.92 us (4%)
  starting transfers between devices  0.97 us (2%)
    pallas_call x2, Pallas kernels, attn_call(): pl.pallas_call(kernel, out_shape=out_shape, grid_spec=grid_spec, compiler...  33.4 us
    slice x3, local copies, waits for them, and re-layouts, length_of(): lo = blk[0, c_rows + s_rows, 1].astype(jnp.int32)  2.53 us
    concatenate x1, other arithmetic, body(): merged = jnp.concatenate([cache_kv, span_kv, tag], axis=1)  2.07 us
    ppermute x3, waiting for transfers between devices, send(): return lax.ppermute(x, 'seq', [(i, fn(i)) for i in range(n)])  1.92 us
    unnamed x4, local copies, waits for them, and re-layouts  1.79 us
    concatenate x2, local copies, waits for them, and re-layouts, run(): sc = jnp.concatenate(lens + origins + [own.reshape(1)]).astype(jnp.int32)  1.27 us
  transfers between devices with their start and end apart: 3, of which 1 were waited for; matrix products, arithmetic and copies ran while one was open for 5% of the time, Pallas kernels for 34%

profile of v1, /device:TPU:13, one launch (start us, length us, event | category | flops | bytes accessed | tf_op | source)
XLA Modules:
  0.0 48.8 jit_solution(5990389163885712053)
XLA Ops:
  0.7 0.1 scatter.9
  0.8 2.1 %pad_maximum_fusion = bf16[2,784,256]{2,1,0:T(8,128)(2,1)} fusion(bf16[2,16,256]{2,1,0:T(8,128)(2,1)S(1)} %scatter.9, bf16[2,256,256]{2,1,0:T(8,128)(2,1)} %refs_1_.1, bf16[2,512,256]{2,1,0:T(8,128)(2,1)} %refs_0_.1), kind=kLoop, calls=%fused_computation | loop fusion | flops 2408448 | bytes 1605632 | tf_op jit(solution)/shard_map/concatenate | solution.py:211
  2.9 0.7 %collective-permute-start = (bf16[2,784,256]{2,1,0:T(8,128)(2,1)}, bf16[2,784,256]{2,1,0:T(8,128)(2,1)S(1)}, u32[]{:S(2)}, u32[]{:S(2)}) collective-permute-start(bf16[2,784,256]{2,1,0:T(8,128)(2,1)} %pad_maximum_fusion), channel_id=1, source_target_pairs={{0,4},{4,0},{8,12},{12,8},{1,5},{5,1},{9,13},{13,9},{2,6},{6,2},{1... | collective-permute-start | bytes 2408456 | tf_op jit(solution)/shard_map/ppermute | solution.py:215
  3.6 0.2 collective-permute-start.1
  3.8 1.9 %collective-permute-done.refs_2_.refs_3_ = bf16[2,784,256]{2,1,0:T(8,128)(2,1)S(1)} collective-permute-done((bf16[2,784,256]{2,1,0:T(8,128)(2,1)}, bf16[2,784,256]{2,1,0:T(8,128)(2,1)S(1)}, u32[]{:S(2)}, u32[]{:S(2)}) %collective-permute-start) | collective-permute-done | bytes 802848 | tf_op jit(solution)/shard_map/ppermute | solution.py:215
  5.7 0.0 copy-start.1
  5.7 0.9 %copy-done.1 = bf16[2,784,256]{2,1,0:T(8,128)(2,1)} copy-done((bf16[2,784,256]{2,1,0:T(8,128)(2,1)}, bf16[2,784,256]{2,1,0:T(8,128)(2,1)S(1)}, u32[]{:S(2)}) %copy-start.1) | copy-done | bytes 802840
  6.6 0.6 %fusion.2 = (bf16[1,1,1]{2,1,0:T(2,128)(2,1)}, bf16[1,1,1]{2,1,0:T(2,128)(2,1)}) fusion(bf16[2,784,256]{2,1,0:T(8,128)(2,1)S(1)} %collective-permute-done.refs_2_.refs_3_), kind=kLoop, calls=%fused_computation.3 | loop fusion | bytes 8 | tf_op jit(solution)/shard_map/slice | solution.py:219
  8.5 0.7 %concatenate.15.sc_ref = s32[5]{0:T(128)} concatenate(s32[1]{0:T(128)} %copy.6, s32[1]{0:T(128)} %bitcast.3, s32[1]{0:T(128)} %bitcast.4, s32[1]{0:T(128)} %bitcast.5, s32[1]{0:T(128)} %bitcast.4), dimensions={0} | concatenate | bytes 40 | tf_op jit(solution)/shard_map/concatenate | solution.py:227
  9.2 16.5 %shard_map.46 = (f32[4096,128]{1,0:T(8,128)}, f32[4096,128]{1,0:T(8,128)}, f32[4096,128]{1,0:T(8,128)}) custom-call(s32[5]{0:T(128)} %concatenate.15.sc_ref, bf16[256,2048]{1,0:T(8,128)(2,1)} %q_ref.3, bf16[2,512,256]{2,1,0:T(8,128)(2,1)} %refs_0_.1, bf16[2,256,256]{2,1,0:T(8,128)(2,1)} %refs_1_.1, bf16[2,784,256]{2,1,0:T(8,128)(2,1)} %copy-done.1, ...), custom_call_target="tpu_custom_call" | custom-call | flops 3221225472 | bytes 15204352 | tf_op jit(solution)/shard_map/pallas_call | solution.py:171
  25.7 0.0 collective-permute-done.1.refs_0_.refs_1_
  25.7 0.1 collective-permute-start.2
  25.8 1.3 %fusion.1 = (bf16[1,1,1]{2,1,0:T(2,128)(2,1)}, bf16[1,1,1]{2,1,0:T(2,128)(2,1)}) fusion(bf16[2,784,256]{2,1,0:T(8,128)(2,1)} %collective-permute-done.1.refs_0_.refs_1_), kind=kLoop, calls=%fused_computation.2 | loop fusion | bytes 8 | tf_op jit(solution)/shard_map/slice | solution.py:219
  28.4 0.0 collective-permute-done.2.refs_2_.refs_3_
  28.4 0.0 copy-start
  28.4 0.9 %copy-done = bf16[2,784,256]{2,1,0:T(8,128)(2,1)} copy-done((bf16[2,784,256]{2,1,0:T(8,128)(2,1)}, bf16[2,784,256]{2,1,0:T(8,128)(2,1)S(1)}, u32[]{:S(2)}) %copy-start) | copy-done | bytes 802840
  29.3 0.6 %fusion = (bf16[1,1,1]{2,1,0:T(2,128)(2,1)}, bf16[1,1,1]{2,1,0:T(2,128)(2,1)}) fusion(bf16[2,784,256]{2,1,0:T(8,128)(2,1)S(1)} %collective-permute-done.2.refs_2_.refs_3_), kind=kLoop, calls=%fused_computation.1 | loop fusion | bytes 8 | tf_op jit(solution)/shard_map/slice | solution.py:219
  31.1 0.6 %concatenate.16.sc_ref = s32[5]{0:T(128)} concatenate(s32[1]{0:T(128)} %bitcast.6, s32[1]{0:T(128)} %bitcast.7, s32[1]{0:T(128)} %bitcast.8, s32[1]{0:T(128)} %bitcast.9, s32[1]{0:T(128)} %bitcast.4), dimensions={0} | concatenate | bytes 40 | tf_op jit(solution)/shard_map/concatenate | solution.py:227
  31.7 16.9 %shard_map.47 = bf16[256,2048]{1,0:T(8,128)(2,1)} custom-call(s32[5]{0:T(128)} %concatenate.16.sc_ref, bf16[256,2048]{1,0:T(8,128)(2,1)} %q_ref.3, bf16[2,784,256]{2,1,0:T(8,128)(2,1)} %collective-permute-done.1.refs_0_.refs_1_, bf16[2,784,256]{2,1,0:T(8,128)(2,1)} %collective-permute-done.1.refs_0_.refs_1_, bf16[2,784,256]{2,1,0:T(8,128)(2,1)} %copy-done, ...), custom_call_target="tpu_custom_call" | custom-call | flops 3221225472 | bytes 15204352 | tf_op jit(solution)/shard_map/pallas_call | solution.py:171
  (1 shorter events, 0.0 us)
Async XLA Ops:
  2.9 2.8 %collective-permute-start = (bf16[2,784,256]{2,1,0:T(8,128)(2,1)}, bf16[2,784,256]{2,1,0:T(8,128)(2,1)S(1)}, u32[]{:S(2)}, u32[]{:S(2)}) collective-permute-start(bf16[2,784,256]{2,1,0:T(8,128)(2,1)} %pad_maximum_fusion), channel_id=1, source_target_pairs={{0,4},{4,0},{8,12},{12,8},{1,5},{5,1},{9,13},{13,9},{2,6},{6,2},{1... | collective-permute-start | bytes 2408456 | tf_op jit(solution)/shard_map/ppermute | solution.py:215
  3.6 22.1 %collective-permute-start.1 = (bf16[2,784,256]{2,1,0:T(8,128)(2,1)}, bf16[2,784,256]{2,1,0:T(8,128)(2,1)}, u32[]{:S(2)}, u32[]{:S(2)}) collective-permute-start(bf16[2,784,256]{2,1,0:T(8,128)(2,1)} %pad_maximum_fusion), channel_id=1, source_target_pairs={{0,8},{4,12},{8,0},{12,4},{1,9},{5,13},{9,1},{13,5},{2,10},{6,14},... | collective-permute-start | bytes 2408456 | tf_op jit(solution)/shard_map/ppermute | solution.py:215
  5.7 0.9 %copy-start.1 = (bf16[2,784,256]{2,1,0:T(8,128)(2,1)}, bf16[2,784,256]{2,1,0:T(8,128)(2,1)S(1)}, u32[]{:S(2)}) copy-start(bf16[2,784,256]{2,1,0:T(8,128)(2,1)S(1)} %collective-permute-done.refs_2_.refs_3_) | copy-start | bytes 2408452
  25.7 2.7 %collective-permute-start.2 = (bf16[2,784,256]{2,1,0:T(8,128)(2,1)}, bf16[2,784,256]{2,1,0:T(8,128)(2,1)S(1)}, u32[]{:S(2)}, u32[]{:S(2)}) collective-permute-start(bf16[2,784,256]{2,1,0:T(8,128)(2,1)} %collective-permute-done.1.refs_0_.refs_1_), channel_id=1, source_target_pairs={{0,4},{4,0},{8,12},{12,8},{1,5},{5,1},{9,13},{13,9},{2,6},{6,2},{1... | collective-permute-start | bytes 2408456 | tf_op jit(solution)/shard_map/ppermute | solution.py:215
  28.4 0.9 %copy-start = (bf16[2,784,256]{2,1,0:T(8,128)(2,1)}, bf16[2,784,256]{2,1,0:T(8,128)(2,1)S(1)}, u32[]{:S(2)}) copy-start(bf16[2,784,256]{2,1,0:T(8,128)(2,1)S(1)} %collective-permute-done.2.refs_2_.refs_3_) | copy-start | bytes 2408452

commit v2 on v0

--- a/solution.py
+++ b/solution.py
@@ -182,26 +182,16 @@
     n_chips = n // 2
     c_rows = cache_kv.shape[1]
     s_rows = span_kv.shape[1]
-    kv_width = cache_kv.shape[2]
-    length = cache_len.reshape(())
-    tag = jnp.zeros((2, 16, kv_width), cache_kv.dtype)
-    tag = tag.at[0, 0, 0].set((length // 64).astype(cache_kv.dtype))
-    tag = tag.at[0, 0, 1].set((length % 64).astype(cache_kv.dtype))
-    merged = jnp.concatenate([cache_kv, span_kv, tag], axis=1)
+    merged = jnp.concatenate([cache_kv, span_kv], axis=1)
     srow = c_rows // s_rows
 
     def send(x, fn):
         return lax.ppermute(x, "seq", [(i, fn(i)) for i in range(n)])
 
-    def length_of(blk):
-        hi = blk[0, c_rows + s_rows, 0].astype(jnp.int32)
-        lo = blk[0, c_rows + s_rows, 1].astype(jnp.int32)
-        return hi * 64 + lo
-
     calls = [0]
 
     def run(phase, state):
-        lens = [jnp.asarray(ln, jnp.int32).reshape(1) for _, ln, _ in phase]
+        lens = [ln.reshape(1) for _, ln, _ in phase]
         origins = [jnp.asarray(o, jnp.int32).reshape(1) for _, _, o in phase]
         sc = jnp.concatenate(lens + origins + [own.reshape(1)]).astype(jnp.int32)
         insts = [b for b, _, _ in phase]
@@ -209,7 +199,7 @@
         calls[0] += 1
         return attn_call(sc, query_rows, insts, (c_rows, s_rows), state, first=first, last=(calls[0] == n_chips))
 
-    part = send(merged, lambda i: i ^ 1)
+    part_len = send(cache_len, lambda i: i ^ 1)
     k_right = n_chips // 2
     k_left = n_chips - 1 - k_right
     hops = []
@@ -217,13 +207,19 @@
         blk = merged
         for k in range(1, count + 1):
             blk = send(blk, lambda i, sign=sign: (i + sign) % n)
-            hops.append((blk, sign, k))
-    state = run([((cache_kv, span_kv, 0), length, own), ((part, part, srow), length_of(part), own ^ 1)], None)
-    for blk, sign, k in hops:
+            shift = sign * k
+            far_len = send(cache_len, lambda i, shift=shift: (i + shift) % n)
+            fwd_len = send(cache_len, lambda i, shift=shift: ((i + shift) % n) ^ 1)
+            hops.append((blk, far_len, fwd_len, sign, k))
+    part = send(merged, lambda i: i ^ 1)
+    part_len, lens_later = lax.optimization_barrier((part_len, [(h[1], h[2]) for h in hops]))
+    hops = [(h[0], fl, wl, h[3], h[4]) for h, (fl, wl) in zip(hops, lens_later)]
+    state = run([((cache_kv, span_kv, 0), cache_len, own), ((part, part, srow), part_len, own ^ 1)], None)
+    for blk, far_len, fwd_len, sign, k in hops:
         state, blk = lax.optimization_barrier((state, blk))
         origin = (own - sign * k) % n
         fwd = send(blk, lambda i: i ^ 1)
-        state = run([((blk, blk, srow), length_of(blk), origin), ((fwd, fwd, srow), length_of(fwd), origin ^ 1)], state)
+        state = run([((blk, blk, srow), far_len, origin), ((fwd, fwd, srow), fwd_len, origin ^ 1)], state)
     return state
 
 

time: 43.5 us -> 56.5 us (1.30)
  the two profiles are of different devices: /device:TPU:13 before, /device:TPU:31 now
where the time goes in v2:
time: 56.5 us; the launch traced here: 56.2 us
  Pallas kernels  28.4 us (50%)
  waiting for transfers between devices  17 us (30%)
  local copies, waits for them, and re-layouts  6.94 us (12%)
  starting transfers between devices  3.03 us (5%)
  between operations  0.74 us (1%)
    pallas_call x2, Pallas kernels, attn_call(): pl.pallas_call(kernel, out_shape=out_shape, grid_spec=grid_spec, compiler...  28.4 us
    ppermute x6, waiting for transfers between devices, send(): return lax.ppermute(x, 'seq', [(i, fn(i)) for i in range(n)])  17 us
    concatenate x2, local copies, waits for them, and re-layouts, run(): sc = jnp.concatenate(lens + origins + [own.reshape(1)]).astype(jnp.int32)  3.12 us
    ppermute x6, starting transfers between devices, send(): return lax.ppermute(x, 'seq', [(i, fn(i)) for i in range(n)])  3.03 us
    unnamed x7, local copies, waits for them, and re-layouts  2.84 us
  transfers between devices with their start and end apart: 6, of which 3 were waited for; matrix products, arithmetic and copies ran while one was open for 6% of the time, Pallas kernels for 25%

profile of v2, /device:TPU:31, one launch (start us, length us, event | category | flops | bytes accessed | tf_op | source)
XLA Modules:
  0.0 56.2 jit_solution(8876710177999190877)
XLA Ops:
  0.0 1.1 %constant_dynamic-update-slice_fusion.1 = bf16[2,768,256]{2,1,0:T(8,128)(2,1)S(1)} fusion(bf16[2,512,256]{2,1,0:T(8,128)(2,1)} %refs_1_.1), kind=kLoop, calls=%fused_computation.1 | loop fusion | bytes 1048576
  1.1 1.0 %constant_dynamic-update-slice_fusion = bf16[2,768,256]{2,1,0:T(8,128)(2,1)S(1)} fusion(bf16[2,768,256]{2,1,0:T(8,128)(2,1)S(1)} %constant_dynamic-update-slice_fusion.1, bf16[2,256,256]{2,1,0:T(8,128)(2,1)} %refs_3_.1), kind=kLoop, calls=%fused_computation | loop fusion | bytes 524288 | tf_op jit(solution)/shard_map/concatenate | solution.py:185
  2.1 0.7 %collective-permute-start.3 = (bf16[2,768,256]{2,1,0:T(8,128)(2,1)S(1)}, bf16[2,768,256]{2,1,0:T(8,128)(2,1)S(1)}, u32[]{:S(2)}, u32[]{:S(2)}) collective-permute-start(bf16[2,768,256]{2,1,0:T(8,128)(2,1)S(1)} %constant_dynamic-update-slice_fusion), channel_id=1, source_target_pairs={{0,4},{4,0},{8,12},{12,8},{1,5},{5,1},{9,13},{13,9},{2,6},{6,2},{1... | collective-permute-start | bytes 2359304 | tf_op jit(solution)/shard_map/ppermute | solution.py:189
  2.8 0.2 collective-permute-start.4
  3.0 1.2 %collective-permute-start.1 = (s32[1]{0:T(128)}, s32[1]{0:T(128)}, u32[]{:S(2)}, u32[]{:S(2)}) collective-permute-start(s32[1]{0:T(128)} %param.7), channel_id=1, source_target_pairs={{0,8},{4,12},{8,0},{12,4},{1,9},{5,13},{9,1},{13,5},{2,10},{6,14},... | collective-permute-start | bytes 20 | tf_op jit(solution)/shard_map/ppermute | solution.py:189
  4.3 0.6 %collective-permute-start = (s32[1]{0:T(128)}, s32[1]{0:T(128)}, u32[]{:S(2)}, u32[]{:S(2)}) collective-permute-start(s32[1]{0:T(128)} %param.7), channel_id=1, source_target_pairs={{0,4},{4,0},{8,12},{12,8},{1,5},{5,1},{9,13},{13,9},{2,6},{6,2},{1... | collective-permute-start | bytes 20 | tf_op jit(solution)/shard_map/ppermute | solution.py:189
  4.9 0.1 collective-permute-start.2
  5.7 16.2 %collective-permute-done.1 = s32[1]{0:T(128)} collective-permute-done((s32[1]{0:T(128)}, s32[1]{0:T(128)}, u32[]{:S(2)}, u32[]{:S(2)}) %collective-permute-start.1) | collective-permute-done | bytes 36 | tf_op jit(solution)/shard_map/ppermute | solution.py:189
  21.9 0.0 collective-permute-done
  21.9 0.4 collective-permute-done.2
  22.4 1.2 %concatenate.10.sc_ref = s32[5]{0:T(128)} concatenate(s32[1]{0:T(128)S(6)} %copy.6, s32[1]{0:T(128)} %collective-permute-done, s32[1]{0:T(128)} %bitcast.2, s32[1]{0:T(128)} %bitcast.3, s32[1]{0:T(128)} %bitcast.2), dimensions={0} | concatenate | bytes 40 | tf_op jit(solution)/shard_map/concatenate | solution.py:196
  23.6 0.0 collective-permute-done.3.refs_4_.refs_5_.refs_6_.refs_7_
  23.6 0.0 copy-start.2
  23.6 0.9 %copy-done.2 = bf16[2,768,256]{2,1,0:T(8,128)(2,1)} copy-done((bf16[2,768,256]{2,1,0:T(8,128)(2,1)}, bf16[2,768,256]{2,1,0:T(8,128)(2,1)S(1)}, u32[]{:S(2)}) %copy-start.2) | copy-done | bytes 786456
  24.5 13.8 %shard_map.46 = (f32[4096,128]{1,0:T(8,128)}, f32[4096,128]{1,0:T(8,128)}, f32[4096,128]{1,0:T(8,128)}) custom-call(s32[5]{0:T(128)} %concatenate.10.sc_ref, bf16[256,2048]{1,0:T(8,128)(2,1)} %q_ref.3, bf16[2,512,256]{2,1,0:T(8,128)(2,1)} %refs_1_.1, bf16[2,512,256]{2,1,0:T(8,128)(2,1)} %refs_1_.1, bf16[2,256,256]{2,1,0:T(8,128)(2,1)} %refs_3_.1, ...), custom_call_target="tpu_custom_call" | custom-call | flops 3221225472 | bytes 15204352 | tf_op jit(solution)/shard_map/pallas_call | solution.py:150
  38.3 0.0 collective-permute-done.4.refs_0_.refs_1_.refs_2_.refs_3_
  38.3 0.0 copy-start
  38.4 0.1 collective-permute-start.5
  38.5 1.9 %concatenate.9.sc_ref = s32[5]{0:T(128)} concatenate(s32[1]{0:T(128)} %collective-permute-done.1, s32[1]{0:T(128)} %collective-permute-done.2, s32[1]{0:T(128)} %bitcast, s32[1]{0:T(128)} %bitcast.1, s32[1]{0:T(128)} %bitcast.2), dimensions={0} | concatenate | bytes 40 | tf_op jit(solution)/shard_map/concatenate | solution.py:196
  40.3 0.4 collective-permute-done.5.refs_4_.refs_5_.refs_6_.refs_7_
  40.7 0.0 copy-done
  40.7 0.0 copy-start.1
  40.7 0.9 %copy-done.1 = bf16[2,768,256]{2,1,0:T(8,128)(2,1)} copy-done((bf16[2,768,256]{2,1,0:T(8,128)(2,1)}, bf16[2,768,256]{2,1,0:T(8,128)(2,1)S(1)}, u32[]{:S(2)}) %copy-start.1) | copy-done | bytes 786456
  41.6 14.6 %shard_map.47 = bf16[256,2048]{1,0:T(8,128)(2,1)} custom-call(s32[5]{0:T(128)} %concatenate.9.sc_ref, bf16[256,2048]{1,0:T(8,128)(2,1)} %q_ref.3, bf16[2,768,256]{2,1,0:T(8,128)(2,1)} %copy-done, bf16[2,768,256]{2,1,0:T(8,128)(2,1)} %copy-done, bf16[2,768,256]{2,1,0:T(8,128)(2,1)} %copy-done, bf16[2,768,256]{2,1,0:T(8,128)(2,1)} %copy-done, ...), custom_call_target="tpu_custom_call" | custom-call | flops 3221225472 | bytes 15204352 | tf_op jit(solution)/shard_map/pallas_call | solution.py:150
Async XLA Ops:
  2.1 21.6 %collective-permute-start.3 = (bf16[2,768,256]{2,1,0:T(8,128)(2,1)S(1)}, bf16[2,768,256]{2,1,0:T(8,128)(2,1)S(1)}, u32[]{:S(2)}, u32[]{:S(2)}) collective-permute-start(bf16[2,768,256]{2,1,0:T(8,128)(2,1)S(1)} %constant_dynamic-update-slice_fusion), channel_id=1, source_target_pairs={{0,4},{4,0},{8,12},{12,8},{1,5},{5,1},{9,13},{13,9},{2,6},{6,2},{1... | collective-permute-start | bytes 2359304 | tf_op jit(solution)/shard_map/ppermute | solution.py:189
  2.8 35.6 %collective-permute-start.4 = (bf16[2,768,256]{2,1,0:T(8,128)(2,1)S(1)}, bf16[2,768,256]{2,1,0:T(8,128)(2,1)S(1)}, u32[]{:S(2)}, u32[]{:S(2)}) collective-permute-start(bf16[2,768,256]{2,1,0:T(8,128)(2,1)S(1)} %constant_dynamic-update-slice_fusion), channel_id=1, source_target_pairs={{0,8},{4,12},{8,0},{12,4},{1,9},{5,13},{9,1},{13,5},{2,10},{6,14},... | collective-permute-start | bytes 2359304 | tf_op jit(solution)/shard_map/ppermute | solution.py:189
  3.0 18.9 %collective-permute-start.1 = (s32[1]{0:T(128)}, s32[1]{0:T(128)}, u32[]{:S(2)}, u32[]{:S(2)}) collective-permute-start(s32[1]{0:T(128)} %param.7), channel_id=1, source_target_pairs={{0,8},{4,12},{8,0},{12,4},{1,9},{5,13},{9,1},{13,5},{2,10},{6,14},... | collective-permute-start | bytes 20 | tf_op jit(solution)/shard_map/ppermute | solution.py:189
  4.3 17.6 %collective-permute-start = (s32[1]{0:T(128)}, s32[1]{0:T(128)}, u32[]{:S(2)}, u32[]{:S(2)}) collective-permute-start(s32[1]{0:T(128)} %param.7), channel_id=1, source_target_pairs={{0,4},{4,0},{8,12},{12,8},{1,5},{5,1},{9,13},{13,9},{2,6},{6,2},{1... | collective-permute-start | bytes 20 | tf_op jit(solution)/shard_map/ppermute | solution.py:189
  4.9 17.5 %collective-permute-start.2 = (s32[1]{0:T(128)}, s32[1]{0:T(128)}, u32[]{:S(2)}, u32[]{:S(2)}) collective-permute-start(s32[1]{0:T(128)} %param.7), channel_id=1, source_target_pairs={{0,12},{4,8},{8,4},{12,0},{1,13},{5,9},{9,5},{13,1},{2,14},{6,10},... | collective-permute-start | bytes 20 | tf_op jit(solution)/shard_map/ppermute | solution.py:189
  23.6 0.9 %copy-start.2 = (bf16[2,768,256]{2,1,0:T(8,128)(2,1)}, bf16[2,768,256]{2,1,0:T(8,128)(2,1)S(1)}, u32[]{:S(2)}) copy-start(bf16[2,768,256]{2,1,0:T(8,128)(2,1)S(1)} %collective-permute-done.3.refs_4_.refs_5_.refs_6_.refs_7_) | copy-start | bytes 2359300
  38.3 2.4 %copy-start = (bf16[2,768,256]{2,1,0:T(8,128)(2,1)}, bf16[2,768,256]{2,1,0:T(8,128)(2,1)S(1)}, u32[]{:S(2)}) copy-start(bf16[2,768,256]{2,1,0:T(8,128)(2,1)S(1)} %collective-permute-done.4.refs_0_.refs_1_.refs_2_.refs_3_) | copy-start | bytes 2359300
  38.4 2.4 %collective-permute-start.5 = (bf16[2,768,256]{2,1,0:T(8,128)(2,1)S(1)}, bf16[2,768,256]{2,1,0:T(8,128)(2,1)S(1)}, u32[]{:S(2)}, u32[]{:S(2)}) collective-permute-start(bf16[2,768,256]{2,1,0:T(8,128)(2,1)S(1)} %collective-permute-done.4.refs_0_.refs_1_.refs_2_.refs_3_), channel_id=1, source_target_pairs={{0,4},{4,0},{8,12},{12,8},{1,5},{5,1},{9,13},{13,9},{2,6},{6,2},{1... | collective-permute-start | bytes 2359304 | tf_op jit(solution)/shard_map/ppermute | solution.py:189
  40.7 0.9 %copy-start.1 = (bf16[2,768,256]{2,1,0:T(8,128)(2,1)}, bf16[2,768,256]{2,1,0:T(8,128)(2,1)S(1)}, u32[]{:S(2)}) copy-start(bf16[2,768,256]{2,1,0:T(8,128)(2,1)S(1)} %collective-permute-done.5.refs_4_.refs_5_.refs_6_.refs_7_) | copy-start | bytes 2359300
